TPU v7x, 512 devices: a whole 4x8x8 slice. The times are simulated.
512 devices in a mesh: seq: 128 (over y, z, core), head: 4 (over x).
Axes of the slice: x: 4, y: 8, z: 8, core: 2. Of those that a mesh axis runs over, the one named last changes fastest.
Arguments:
- out_grad: bfloat16 [16384, 4096], P('seq', 'head'), may hold values from -6 to 6
- expert_ids: int32 [16384, 8], P('seq'), may hold values from 0 to 127, all different within a row; in each aligned block of 128 rows (0 to 127, 128 to 255, ...) at most 12 rows name the same one
- top_logits: float32 [16384, 8], P('seq'), may hold values from -10 to 310
- doc_start: int32 [16384], P('seq'), may hold values from 0 to 16383, as said below
- router: bfloat16 [128, 4096], P(None, 'head'), may hold values from -0.09375 to 0.09375
- w_down: bfloat16 [128, 768, 4096], P('seq', None, 'head'), may hold values from -0.21875 to 0.21875
- saved_gu: bfloat16 [128, 2, 768, 1536], P('seq', None, 'head'), may hold values from -6 to 6
- out_weight: bfloat16 [4096, 4096], P('head', 'seq'), may hold values from -0.09375 to 0.09375
- query: bfloat16 [16384, 32, 128], P('seq', 'head'), may hold values from -64 to 64
- key: bfloat16 [16384, 4, 128], P('seq', 'head'), may hold values from -8 to 8
- value: bfloat16 [16384, 4, 128], P('seq', 'head'), may hold values from -6 to 6
Outputs:
- gate_up_grad: bfloat16 [128, 2, 768, 1536], P('seq', None, 'head')
- route_grad: float32 [16384, 8], P('seq')
- query_grad: bfloat16 [16384, 32, 128], P('seq', 'head')
- key_grad: bfloat16 [16384, 4, 128], P('seq', 'head')
- value_grad: bfloat16 [16384, 4, 128], P('seq', 'head')
Inputs may be any that keep to these rules, and one draw needn't show every extreme that they name: `expert_ids`: each token names 8 different experts; among the 128 tokens of one index of seq no expert is named by more than 12 tokens. doc_start[t] is the first position of the document that holds t; documents lie end to end, each has at most 896 tokens and one has exactly 896.
All inputs are finite; a program needn't handle non-finite values.
Results may differ from a plain program's by a relative error of at most 0.03.
Values may be sent and summed in bfloat16 or wider, within the bound.
No kernel may reach another device: no remote copies, remote signals or barrier semaphores. Data moves between devices by JAX's collectives and lax.ppermute only.
A program may use at most 128 MiB of HBM per device.

v0:
```python
import jax
import jax.numpy as jnp
from jax import lax
from jax.sharding import PartitionSpec as P

REACH = 7
masked_score = -1e30
highest = lax.Precision.HIGHEST


def passed_along(array, axis, by):
    count = lax.axis_size(axis)
    pairs = [(i, i + by) for i in range(count) if 0 <= i + by < count]
    return lax.ppermute(array, axis, pairs)


def attend(queries, upstream, keys_all, values_all, query_pos, key_pos, doc_begin, score_scale):
    scores = (
        jnp.einsum("tkgd,lkd->kgtl", queries, keys_all, preferred_element_type=jnp.float32)
        * score_scale
    )
    valid = (key_pos[None, :] <= query_pos[:, None]) & (key_pos[None, :] >= doc_begin[:, None])
    scores = jnp.where(valid[None, None], scores, masked_score)
    row_max = jnp.max(scores, axis=3, keepdims=True)
    exponent = jnp.exp(scores - row_max)
    probs = exponent / jnp.sum(exponent, axis=3, keepdims=True)
    dprob = jnp.einsum("tkgd,lkd->kgtl", upstream, values_all, preferred_element_type=jnp.float32)
    row_dot = jnp.sum(probs * dprob, axis=3, keepdims=True)
    probs_b = probs.astype(jnp.bfloat16)
    dscore = (probs * (dprob - row_dot)).astype(jnp.bfloat16)
    query_part = (
        jnp.einsum("kgtl,lkd->tkgd", dscore, keys_all, preferred_element_type=jnp.float32)
        * score_scale
    )
    key_part = (
        jnp.einsum("kgtl,tkgd->lkd", dscore, queries, preferred_element_type=jnp.float32)
        * score_scale
    )
    value_part = jnp.einsum("kgtl,tkgd->lkd", probs_b, upstream, preferred_element_type=jnp.float32)
    return (query_part, key_part, value_part)


def per_device(
    out_grad,
    expert_ids,
    top_logits,
    doc_start,
    router,
    w_down,
    saved_gu,
    out_weight,
    query,
    key,
    value,
):
    seq_count = lax.axis_size("seq")
    seq_index = lax.axis_index("seq")
    tokens_here = out_grad.shape[0]
    features = out_grad.shape[1]
    slots_all = saved_gu.shape[3]
    capacity = slots_all // seq_count
    experts = router.shape[0]
    top_count = expert_ids.shape[1]
    weights = jax.nn.softmax(top_logits, axis=1)
    hits = (expert_ids[:, :, None] == jnp.arange(experts, dtype=jnp.int32)[None, None, :]).astype(
        jnp.float32
    )
    per_token = jnp.sum(hits, axis=1)
    earlier = (jnp.arange(tokens_here)[:, None] > jnp.arange(tokens_here)[None, :]).astype(
        jnp.float32
    )
    before = jnp.dot(earlier, per_token, precision=highest)
    rank = jnp.sum(hits * before[:, None, :], axis=2).astype(jnp.int32)
    target = expert_ids * capacity + rank
    placed = (
        target[None, :, :] == jnp.arange(experts * capacity, dtype=jnp.int32)[:, None, None]
    ).astype(jnp.float32)
    pick = jnp.sum(placed, axis=2).astype(jnp.bfloat16)
    send_rows = jnp.dot(pick, out_grad, preferred_element_type=jnp.float32).astype(jnp.bfloat16)
    send_weight = jnp.sum(placed * weights[None, :, :], axis=(1, 2)).astype(jnp.bfloat16)
    weight_lanes = jnp.zeros((experts * capacity, 128), jnp.bfloat16).at[:, 0].set(send_weight)
    payload = jnp.concatenate([send_rows, weight_lanes], axis=1)
    weight_full = out_weight
    kv_heads = key.shape[1]
    head_dim = key.shape[2]
    group = query.shape[1] // kv_heads
    paired = jnp.stack([key, value])
    blocks = [paired]
    for distance in range(1, REACH + 1):
        blocks.append(passed_along(paired, "seq", distance))
    sent_payload = lax.all_to_all(
        payload.reshape(experts, capacity, features + 128),
        "seq",
        split_axis=0,
        concat_axis=0,
        tiled=True,
    ).reshape(slots_all, features + 128)
    sent_payload, weight_full, blocks = lax.optimization_barrier(
        (sent_payload, weight_full, tuple(blocks))
    )
    slot_rows = sent_payload[:, :features]
    sent_weight = sent_payload[:, features]
    weight_here = w_down[0]
    raw = lax.psum_scatter(
        lax.dot_general(
            weight_here, slot_rows, (((1,), (1,)), ((), ())), preferred_element_type=jnp.float32
        ).astype(jnp.bfloat16),
        "head",
        scatter_dimension=0,
        tiled=True,
    ).astype(jnp.float32)
    gate = saved_gu[0, 0].astype(jnp.float32)
    up = saved_gu[0, 1].astype(jnp.float32)
    sig = jax.nn.sigmoid(gate)
    act = gate * sig
    hidden = act * up
    slot_part = jnp.sum(hidden * raw, axis=0)
    scaled = raw * sent_weight.reshape(slots_all).astype(jnp.float32)[None, :]
    gate_up_grad = jnp.stack([scaled * up * sig * (1.0 + gate * (1.0 - sig)), scaled * act])[
        None
    ].astype(jnp.bfloat16)
    slot_grad = lax.psum(slot_part, "head")
    returned = lax.all_to_all(
        slot_grad.reshape(seq_count, capacity), "seq", split_axis=0, concat_axis=0, tiled=True
    )
    route_grad = jnp.take(returned.reshape(-1), target.reshape(-1)).reshape(tokens_here, top_count)
    logit_grad = weights * (route_grad - jnp.sum(weights * route_grad, axis=1, keepdims=True))
    dense = jnp.einsum("tk,tke->te", logit_grad, hits, precision=highest)
    router_term = jnp.dot(dense, router.astype(jnp.float32), precision=highest)
    input_slice = (out_grad.astype(jnp.float32) + router_term).astype(jnp.bfloat16)
    input_grad = lax.all_gather(input_slice, "head", axis=1, tiled=True)
    core = seq_index % 2
    by_parity = input_grad.reshape(tokens_here, seq_count // 2, 2, -1)
    mine = lax.dynamic_index_in_dim(by_parity, core, axis=2, keepdims=False)
    theirs = lax.dynamic_index_in_dim(by_parity, 1 - core, axis=2, keepdims=False)
    ordered = jnp.concatenate(
        [mine.reshape(tokens_here, -1), theirs.reshape(tokens_here, -1)], axis=1
    )
    attn_grad = lax.dot_general(
        ordered, weight_full, (((1,), (1,)), ((), ())), preferred_element_type=jnp.float32
    ).astype(jnp.bfloat16)
    window = jnp.concatenate(blocks[::-1], axis=1)
    local_pos = jnp.arange(tokens_here, dtype=jnp.int32)
    key_pos = jnp.concatenate(
        [(seq_index - distance) * tokens_here + local_pos for distance in range(REACH, -1, -1)]
    )
    query_pos = seq_index * tokens_here + local_pos
    queries = query.reshape(tokens_here, kv_heads, group, head_dim)
    upstream = attn_grad.reshape(tokens_here, kv_heads, group, head_dim)
    query_part, key_part, value_part = attend(
        queries, upstream, window[0], window[1], query_pos, key_pos, doc_start, head_dim ** (-0.5)
    )
    query_grad = query_part.reshape(query.shape).astype(jnp.bfloat16)
    pieces = jnp.stack([key_part, value_part]).reshape(
        2, REACH + 1, tokens_here, kv_heads, head_dim
    )
    totals = pieces[:, REACH]
    for distance in range(1, REACH + 1):
        totals = totals + passed_along(
            pieces[:, REACH - distance].astype(jnp.bfloat16), "seq", -distance
        ).astype(jnp.float32)
    return (
        gate_up_grad,
        route_grad,
        query_grad,
        totals[0].astype(jnp.bfloat16),
        totals[1].astype(jnp.bfloat16),
    )


def gather_columns(out_weight):
    half = lax.all_gather(out_weight, "chip", axis=1, tiled=True)
    other = lax.ppermute(half, "core", [(0, 1), (1, 0)])
    return jnp.concatenate([half, other], axis=1)


def solution(mesh):
    chips = mesh.devices.shape[0] // 2
    split_mesh = jax.sharding.Mesh(
        mesh.devices.reshape(chips, 2, mesh.devices.shape[1]), ("chip", "core", "head")
    )
    gather = jax.shard_map(
        gather_columns,
        mesh=split_mesh,
        in_specs=P("head", ("chip", "core")),
        out_specs=P("head", ("chip", "core")),
        check_vma=False,
    )
    in_specs = (
        P("seq", "head"),
        P("seq", None),
        P("seq", None),
        P("seq"),
        P(None, "head"),
        P("seq", None, "head"),
        P("seq", None, "head", None),
        P("head", "seq"),
        P("seq", "head", None),
        P("seq", "head", None),
        P("seq", "head", None),
    )
    out_specs = (
        P("seq", None, "head", None),
        P("seq", None),
        P("seq", "head", None),
        P("seq", "head", None),
        P("seq", "head", None),
    )
    body = jax.shard_map(
        per_device, mesh=mesh, in_specs=in_specs, out_specs=out_specs, check_vma=False
    )

    def run(*args):
        args = list(args)
        args[7] = gather(args[7])
        return body(*args)

    return run
```

profile of v0, /device:TPU:49, one launch (start us, length us, event | category | flops | bytes accessed | tf_op | source)
XLA Modules:
  0.0 424.8 jit_solution(11453210561158346732)
XLA Ops:
  13.0 11.6 %convert_reduce_fusion = (bf16[1536,128]{1,0:T(8,128)(2,1)S(1)}, bf16[1536]{0:T(1024)(128)(2,1)S(1)}) fusion(s32[128,8]{0,1:T(8,128)S(1)} %convert_add_fusion, f32[128,8]{0,1:T(8,128)S(1)} %fusion.55), kind=kLoop, calls=%fused_computation.5 | loop fusion | flops 7666176 | bytes 404480 | tf_op jit(solution)/shard_map/reduce_sum | solution.py:78
  29.3 5.8 %copy.130 = bf16[1536,1152]{1,0:T(8,128)(2,1)} copy(bf16[1536,1152]{0,1:T(8,128)(2,1)} %fusion.6) | data formatting | bytes 7077888 | tf_op jit(solution)/shard_map/concatenate | solution.py:82
  35.1 6.5 %reshape.406 = bf16[128,12,1152]{2,1,0:T(8,128)(2,1)} reshape(bf16[1536,1152]{1,0:T(8,128)(2,1)} %copy.130) | data formatting | bytes 7077888 | tf_op jit(solution)/shard_map/reshape | solution.py:92
  41.6 18.2 %all-to-all-start = ((bf16[128,12,1152]{2,1,0:T(8,128)(2,1)}), bf16[128,12,1152]{2,1,0:T(8,128)(2,1)}, u32[]{:S(2)}, u32[]{:S(2)}) async-start(bf16[128,12,1152]{2,1,0:T(8,128)(2,1)} %reshape.406), calls=%async_computation | async-start | bytes 9437184 | tf_op jit(solution)/shard_map/all_to_all | solution.py:91
  59.8 135.4 %all-gather.3.cloned.1.call-done = bf16[1024,2048]{0,1:T(8,128)(2,1)} async-done(((bf16[1024,32]{0,1:T(8,128)(2,1)}), bf16[1024,2048]{0,1:T(8,128)(2,1)}) %all-gather.3.cloned.1.call-update) | async-done | bytes 4194320 | tf_op jit(solution)/shard_map/all_gather | solution.py:172
  195.2 5.7 %collective-permute-start = (bf16[1024,2048]{0,1:T(8,128)(2,1)}, bf16[1024,2048]{0,1:T(8,128)(2,1)}, u32[]{:S(2)}, u32[]{:S(2)}) collective-permute-start(bf16[1024,2048]{0,1:T(8,128)(2,1)} %all-gather.3.cloned.1.call-done), channel_id=1, source_target_pairs={{0,4},{4,0},{1,5},{5,1},{2,6},{6,2},{3,7},{7,3},{8,12},{12,8},{9,1... | collective-permute-start | bytes 12582920 | tf_op jit(solution)/shard_map/ppermute | solution.py:173
  205.5 3.6 collective-permute-start.3
  212.4 6.6 %reshape.407 = bf16[1536,1152]{1,0:T(8,128)(2,1)} reshape(bf16[128,12,1152]{2,1,0:T(8,128)(2,1)} %all-to-all-done) | data formatting | bytes 7077888 | tf_op jit(solution)/shard_map/reshape | solution.py:97
  219.0 5.4 %collective-permute-start.5 = (bf16[2,128,1,128]{3,1,2,0:T(8,128)(2,1)S(1)}, bf16[2,128,1,128]{3,1,2,0:T(8,128)(2,1)S(1)}, u32[]{:S(2)}, u32[]{:S(2)}) collective-permute-start(bf16[2,128,1,128]{3,1,2,0:T(8,128)(2,1)S(1)} %pad_maximum_fusion.3), channel_id=1, source_target_pairs={{0,20},{4,24},{8,28},{12,32},{16,36},{20,40},{24,44},{28,48},{32,5... | collective-permute-start | bytes 196616 | tf_op jit(solution)/shard_map/ppermute | solution.py:14
  226.4 7.1 %collective-permute-start.7 = (bf16[2,128,1,128]{3,1,2,0:T(8,128)(2,1)S(1)}, bf16[2,128,1,128]{3,1,2,0:T(8,128)(2,1)S(1)}, u32[]{:S(2)}, u32[]{:S(2)}) collective-permute-start(bf16[2,128,1,128]{3,1,2,0:T(8,128)(2,1)S(1)} %pad_maximum_fusion.3), channel_id=1, source_target_pairs={{0,28},{4,32},{8,36},{12,40},{16,44},{20,48},{24,52},{28,56},{32,6... | collective-permute-start | bytes 196616 | tf_op jit(solution)/shard_map/ppermute | solution.py:14
  233.5 7.7 %pad_maximum_fusion = bf16[1024,4096]{0,1:T(8,128)(2,1)} fusion(bf16[1024,2048]{0,1:T(8,128)(2,1)} %collective-permute-done, bf16[1024,2048]{0,1:T(8,128)(2,1)} %all-gather.3.cloned.1.call-done), kind=kLoop, calls=%fused_computation.1 | loop fusion | flops 16777216 | bytes 16777216 | tf_op jit(solution)/shard_map/concatenate | solution.py:174
  241.3 6.0 %fusion.9 = bf16[768,1536]{0,1:T(8,128)(2,1)} fusion(bf16[1536,1152]{1,0:T(8,128)(2,1)} %reshape.407, bf16[1,768,1024]{2,1,0:T(8,128)(2,1)S(1)} %copy-done), kind=kOutput, calls=%fused_computation.21 | convolution fusion | flops 2417098752 | bytes 7077888 | tf_op jit(solution)/shard_map/dot_general | solution.py:105
  247.3 4.4 %copy.154 = bf16[768,1536]{1,0:T(8,128)(2,1)} copy(bf16[768,1536]{0,1:T(8,128)(2,1)} %fusion.9) | data formatting | bytes 4718592
  254.8 30.1 %reduce-scatter.4.cloned.1.call-done = bf16[192,1536]{1,0:T(8,128)(2,1)} async-done(((bf16[768,1536]{1,0:T(8,128)(2,1)}), bf16[192,1536]{1,0:T(8,128)(2,1)}) %reduce-scatter.4.cloned.1.call-update) | async-done | bytes 589840
  288.8 12.9 %psum.7 = f32[128,1,12]{2,0,1:T(8,128)} all-reduce(f32[128,1,12]{2,0,1:T(8,128)S(1)} %all_to_all.10), channel_id=1, replica_groups=mesh['chip'=64,'core'=2,'head'=4] {'head'}, use_global_device_ids=true, to_apply=%region_9.0 | all-reduce | flops 1536 | bytes 12288 | tf_op jit(solution)/shard_map/psum | solution.py:122
  301.8 18.3 %all-to-all-start.1 = ((f32[128,1,12]{2,1,0:T(1,128)}), f32[128,1,12]{2,1,0:T(1,128)S(1)}, u32[]{:S(2)}, u32[]{:S(2)}) async-start(f32[128,1,12]{2,1,0:T(1,128)} %bitcast.10), calls=%async_computation.1 | async-start | bytes 131072 | tf_op jit(solution)/shard_map/all_to_all | solution.py:123
  320.4 7.9 %all-to-all-done.1 = f32[128,1,12]{2,1,0:T(1,128)S(1)} async-done(((f32[128,1,12]{2,1,0:T(1,128)}), f32[128,1,12]{2,1,0:T(1,128)S(1)}, u32[]{:S(2)}, u32[]{:S(2)}) %all-to-all-start.1) | async-done | bytes 6176 | tf_op jit(solution)/shard_map/all_to_all | solution.py:123
  329.8 6.2 %gather_fusion = f32[1024]{0:T(1024)S(1)} fusion(f32[1536]{0:T(1024)S(1)} %reshape.408, s32[1024]{0:T(1024)S(1)} %broadcast_clamp_fusion), kind=kCustom, calls=%fused_computation | custom fusion | bytes 12288 | tf_op jit(solution)/shard_map/jit(_take)/gather | solution.py:126
  341.9 17.5 %all-gather.5.cloned.1.call-done = bf16[128,4096]{1,0:T(8,128)(2,1)} async-done(((bf16[128,1024]{1,0:T(8,128)(2,1)}), bf16[128,4096]{1,0:T(8,128)(2,1)}) %all-gather.5.cloned.1.call-update) | async-done | bytes 1048592 | tf_op jit(solution)/shard_map/all_gather | solution.py:131
  361.2 4.8 %convolution_convert_fusion.2 = bf16[128,1024]{1,0:T(8,128)(2,1)S(1)} fusion(bf16[1024,4096]{0,1:T(8,128)(2,1)} %pad_maximum_fusion, bf16[128,2048]{0,1:T(8,128)(2,1)S(1)} %bitcast.183, bf16[128,2048]{0,1:T(8,128)(2,1)S(1)} %bitcast.182), kind=kOutput, calls=%fused_computation.51 | convolution fusion | flops 1075970048 | bytes 9699328 | tf_op jit(solution)/shard_map/dot_general | solution.py:139
  370.8 4.2 copy.142
  380.6 9.3 %collective-permute-start.14 = (bf16[2,128,1,128]{3,1,2,0:T(8,128)(2,1)}, bf16[2,128,1,128]{3,1,2,0:T(8,128)(2,1)}, u32[]{:S(2)}, u32[]{:S(2)}) collective-permute-start(bf16[2,128,1,128]{3,1,2,0:T(8,128)(2,1)} %get-tuple-element.82), channel_id=1, source_target_pairs={{28,0},{32,4},{36,8},{40,12},{44,16},{48,20},{52,24},{56,28},{60,3... | collective-permute-start | bytes 196616 | tf_op jit(solution)/shard_map/ppermute | solution.py:14
  395.8 5.2 %collective-permute-start.12 = (bf16[2,128,1,128]{3,1,0,2:T(8,128)(2,1)S(1)}, bf16[2,128,1,128]{3,1,0,2:T(8,128)(2,1)S(1)}, u32[]{:S(2)}, u32[]{:S(2)}) collective-permute-start(bf16[2,128,1,128]{3,1,0,2:T(8,128)(2,1)S(1)} %get-tuple-element.84), channel_id=1, source_target_pairs={{20,0},{24,4},{28,8},{32,12},{36,16},{40,20},{44,24},{48,28},{52,3... | collective-permute-start | bytes 196616 | tf_op jit(solution)/shard_map/ppermute | solution.py:14
  404.6 4.4 %collective-permute-start.10 = (bf16[2,128,1,128]{3,1,0,2:T(8,128)(2,1)S(1)}, bf16[2,128,1,128]{3,1,0,2:T(8,128)(2,1)S(1)}, u32[]{:S(2)}, u32[]{:S(2)}) collective-permute-start(bf16[2,128,1,128]{3,1,0,2:T(8,128)(2,1)S(1)} %get-tuple-element.86), channel_id=1, source_target_pairs={{12,0},{16,4},{20,8},{24,12},{28,16},{32,20},{36,24},{40,28},{44,3... | collective-permute-start | bytes 196616 | tf_op jit(solution)/shard_map/ppermute | solution.py:14
  (160 shorter events, 65.2 us)
Async XLA Ops:
  7.2 234.1 %copy-start = (bf16[1,768,1024]{2,1,0:T(8,128)(2,1)S(1)}, bf16[1,768,1024]{2,1,0:T(8,128)(2,1)}, u32[]{:S(2)}) copy-start(bf16[1,768,1024]{2,1,0:T(8,128)(2,1)} %param.19) | copy-start | bytes 4718596
  7.2 188.0 %all-gather.3.cloned.1.call-start = ((), (), s32[]{:S(2)}) async-start(), calls=%async_computation.3 | async-start | bytes 4259840 | tf_op jit(solution)/shard_map/all_gather | solution.py:172
  41.6 159.4 %copy-start.26 = (bf16[128,1,128]{2,0,1:T(8,128)(2,1)S(1)}, bf16[128,1,128]{2,0,1:T(8,128)(2,1)}, u32[]{:S(2)}) copy-start(bf16[128,1,128]{2,0,1:T(8,128)(2,1)} %param.24) | copy-start | bytes 98308
  41.6 159.4 %copy-start.27 = (bf16[128,1,128]{2,0,1:T(8,128)(2,1)S(1)}, bf16[128,1,128]{2,0,1:T(8,128)(2,1)}, u32[]{:S(2)}) copy-start(bf16[128,1,128]{2,0,1:T(8,128)(2,1)} %param.23) | copy-start | bytes 98308
  41.6 170.8 %all-to-all-start = ((bf16[128,12,1152]{2,1,0:T(8,128)(2,1)}), bf16[128,12,1152]{2,1,0:T(8,128)(2,1)}, u32[]{:S(2)}, u32[]{:S(2)}) async-start(bf16[128,12,1152]{2,1,0:T(8,128)(2,1)} %reshape.406), calls=%async_computation | async-start | bytes 9437184 | tf_op jit(solution)/shard_map/all_to_all | solution.py:91
  59.7 225.1 %reduce-scatter.4.cloned.1.call-start = ((), (), s32[]{:S(2)}) async-start(), calls=%async_computation.5 | async-start | bytes 2949120
  195.2 31.2 %collective-permute-start = (bf16[1024,2048]{0,1:T(8,128)(2,1)}, bf16[1024,2048]{0,1:T(8,128)(2,1)}, u32[]{:S(2)}, u32[]{:S(2)}) collective-permute-start(bf16[1024,2048]{0,1:T(8,128)(2,1)} %all-gather.3.cloned.1.call-done), channel_id=1, source_target_pairs={{0,4},{4,0},{1,5},{5,1},{2,6},{6,2},{3,7},{7,3},{8,12},{12,8},{9,1... | collective-permute-start | bytes 12582920 | tf_op jit(solution)/shard_map/ppermute | solution.py:173
  201.0 18.1 %collective-permute-start.1 = (bf16[2,128,1,128]{3,1,2,0:T(8,128)(2,1)S(1)}, bf16[2,128,1,128]{3,1,2,0:T(8,128)(2,1)S(1)}, u32[]{:S(2)}, u32[]{:S(2)}) collective-permute-start(bf16[2,128,1,128]{3,1,2,0:T(8,128)(2,1)S(1)} %pad_maximum_fusion.3), channel_id=1, source_target_pairs={{0,4},{4,8},{8,12},{12,16},{16,20},{20,24},{24,28},{28,32},{32,36}... | collective-permute-start | bytes 196616 | tf_op jit(solution)/shard_map/ppermute | solution.py:14
  203.5 21.0 %collective-permute-start.2 = (bf16[2,128,1,128]{3,1,2,0:T(8,128)(2,1)S(1)}, bf16[2,128,1,128]{3,1,2,0:T(8,128)(2,1)S(1)}, u32[]{:S(2)}, u32[]{:S(2)}) collective-permute-start(bf16[2,128,1,128]{3,1,2,0:T(8,128)(2,1)S(1)} %pad_maximum_fusion.3), channel_id=1, source_target_pairs={{0,8},{4,12},{8,16},{12,20},{16,24},{20,28},{24,32},{28,36},{32,40... | collective-permute-start | bytes 196616 | tf_op jit(solution)/shard_map/ppermute | solution.py:14
  205.5 35.7 %collective-permute-start.3 = (bf16[2,128,1,128]{3,1,2,0:T(8,128)(2,1)S(1)}, bf16[2,128,1,128]{3,1,2,0:T(8,128)(2,1)S(1)}, u32[]{:S(2)}, u32[]{:S(2)}) collective-permute-start(bf16[2,128,1,128]{3,1,2,0:T(8,128)(2,1)S(1)} %pad_maximum_fusion.3), channel_id=1, source_target_pairs={{0,12},{4,16},{8,20},{12,24},{16,28},{20,32},{24,36},{28,40},{32,4... | collective-permute-start | bytes 196616 | tf_op jit(solution)/shard_map/ppermute | solution.py:14
  209.2 32.0 %collective-permute-start.4 = (bf16[2,128,1,128]{3,1,2,0:T(8,128)(2,1)S(1)}, bf16[2,128,1,128]{3,1,2,0:T(8,128)(2,1)S(1)}, u32[]{:S(2)}, u32[]{:S(2)}) collective-permute-start(bf16[2,128,1,128]{3,1,2,0:T(8,128)(2,1)S(1)} %pad_maximum_fusion.3), channel_id=1, source_target_pairs={{0,16},{4,20},{8,24},{12,28},{16,32},{20,36},{24,40},{28,44},{32,4... | collective-permute-start | bytes 196616 | tf_op jit(solution)/shard_map/ppermute | solution.py:14
  219.0 22.2 %collective-permute-start.5 = (bf16[2,128,1,128]{3,1,2,0:T(8,128)(2,1)S(1)}, bf16[2,128,1,128]{3,1,2,0:T(8,128)(2,1)S(1)}, u32[]{:S(2)}, u32[]{:S(2)}) collective-permute-start(bf16[2,128,1,128]{3,1,2,0:T(8,128)(2,1)S(1)} %pad_maximum_fusion.3), channel_id=1, source_target_pairs={{0,20},{4,24},{8,28},{12,32},{16,36},{20,40},{24,44},{28,48},{32,5... | collective-permute-start | bytes 196616 | tf_op jit(solution)/shard_map/ppermute | solution.py:14
  224.5 16.7 %collective-permute-start.6 = (bf16[2,128,1,128]{3,1,2,0:T(8,128)(2,1)S(1)}, bf16[2,128,1,128]{3,1,2,0:T(8,128)(2,1)S(1)}, u32[]{:S(2)}, u32[]{:S(2)}) collective-permute-start(bf16[2,128,1,128]{3,1,2,0:T(8,128)(2,1)S(1)} %pad_maximum_fusion.3), channel_id=1, source_target_pairs={{0,24},{4,28},{8,32},{12,36},{16,40},{20,44},{24,48},{28,52},{32,5... | collective-permute-start | bytes 196616 | tf_op jit(solution)/shard_map/ppermute | solution.py:14
  226.4 14.8 %collective-permute-start.7 = (bf16[2,128,1,128]{3,1,2,0:T(8,128)(2,1)S(1)}, bf16[2,128,1,128]{3,1,2,0:T(8,128)(2,1)S(1)}, u32[]{:S(2)}, u32[]{:S(2)}) collective-permute-start(bf16[2,128,1,128]{3,1,2,0:T(8,128)(2,1)S(1)} %pad_maximum_fusion.3), channel_id=1, source_target_pairs={{0,28},{4,32},{8,36},{12,40},{16,44},{20,48},{24,52},{28,56},{32,6... | collective-permute-start | bytes 196616 | tf_op jit(solution)/shard_map/ppermute | solution.py:14
  286.2 50.6 %copy-start.8 = (bf16[128,1024]{1,0:T(8,128)(2,1)S(1)}, bf16[128,1024]{1,0:T(8,128)(2,1)}, u32[]{:S(2)}) copy-start(bf16[128,1024]{1,0:T(8,128)(2,1)} %param.14) | copy-start | bytes 786436
  301.8 26.6 %all-to-all-start.1 = ((f32[128,1,12]{2,1,0:T(1,128)}), f32[128,1,12]{2,1,0:T(1,128)S(1)}, u32[]{:S(2)}, u32[]{:S(2)}) async-start(f32[128,1,12]{2,1,0:T(1,128)} %bitcast.10), calls=%async_computation.1 | async-start | bytes 131072 | tf_op jit(solution)/shard_map/all_to_all | solution.py:123
  320.1 39.3 %all-gather.5.cloned.1.call-start = ((), (), s32[]{:S(2)}) async-start(), calls=%async_computation.4 | async-start | bytes 1310720 | tf_op jit(solution)/shard_map/all_gather | solution.py:131
  380.6 28.4 %collective-permute-start.14 = (bf16[2,128,1,128]{3,1,2,0:T(8,128)(2,1)}, bf16[2,128,1,128]{3,1,2,0:T(8,128)(2,1)}, u32[]{:S(2)}, u32[]{:S(2)}) collective-permute-start(bf16[2,128,1,128]{3,1,2,0:T(8,128)(2,1)} %get-tuple-element.82), channel_id=1, source_target_pairs={{28,0},{32,4},{36,8},{40,12},{44,16},{48,20},{52,24},{56,28},{60,3... | collective-permute-start | bytes 196616 | tf_op jit(solution)/shard_map/ppermute | solution.py:14
  390.0 21.1 %collective-permute-start.13 = (bf16[2,128,1,128]{3,1,0,2:T(8,128)(2,1)S(1)}, bf16[2,128,1,128]{3,1,0,2:T(8,128)(2,1)}, u32[]{:S(2)}, u32[]{:S(2)}) collective-permute-start(bf16[2,128,1,128]{3,1,0,2:T(8,128)(2,1)S(1)} %get-tuple-element.83), channel_id=1, source_target_pairs={{24,0},{28,4},{32,8},{36,12},{40,16},{44,20},{48,24},{52,28},{56,3... | collective-permute-start | bytes 196616 | tf_op jit(solution)/shard_map/ppermute | solution.py:14
  395.8 20.5 %collective-permute-start.12 = (bf16[2,128,1,128]{3,1,0,2:T(8,128)(2,1)S(1)}, bf16[2,128,1,128]{3,1,0,2:T(8,128)(2,1)S(1)}, u32[]{:S(2)}, u32[]{:S(2)}) collective-permute-start(bf16[2,128,1,128]{3,1,0,2:T(8,128)(2,1)S(1)} %get-tuple-element.84), channel_id=1, source_target_pairs={{20,0},{24,4},{28,8},{32,12},{36,16},{40,20},{44,24},{48,28},{52,3... | collective-permute-start | bytes 196616 | tf_op jit(solution)/shard_map/ppermute | solution.py:14
  401.0 15.3 %collective-permute-start.11 = (bf16[2,128,1,128]{3,1,0,2:T(8,128)(2,1)S(1)}, bf16[2,128,1,128]{3,1,0,2:T(8,128)(2,1)S(1)}, u32[]{:S(2)}, u32[]{:S(2)}) collective-permute-start(bf16[2,128,1,128]{3,1,0,2:T(8,128)(2,1)S(1)} %get-tuple-element.85), channel_id=1, source_target_pairs={{16,0},{20,4},{24,8},{28,12},{32,16},{36,20},{40,24},{44,28},{48,3... | collective-permute-start | bytes 196616 | tf_op jit(solution)/shard_map/ppermute | solution.py:14
  404.6 11.7 %collective-permute-start.10 = (bf16[2,128,1,128]{3,1,0,2:T(8,128)(2,1)S(1)}, bf16[2,128,1,128]{3,1,0,2:T(8,128)(2,1)S(1)}, u32[]{:S(2)}, u32[]{:S(2)}) collective-permute-start(bf16[2,128,1,128]{3,1,0,2:T(8,128)(2,1)S(1)} %get-tuple-element.86), channel_id=1, source_target_pairs={{12,0},{16,4},{20,8},{24,12},{28,16},{32,20},{36,24},{40,28},{44,3... | collective-permute-start | bytes 196616 | tf_op jit(solution)/shard_map/ppermute | solution.py:14
  409.0 7.3 %collective-permute-start.9 = (bf16[2,128,1,128]{3,1,0,2:T(8,128)(2,1)S(1)}, bf16[2,128,1,128]{3,1,0,2:T(8,128)(2,1)S(1)}, u32[]{:S(2)}, u32[]{:S(2)}) collective-permute-start(bf16[2,128,1,128]{3,1,0,2:T(8,128)(2,1)S(1)} %get-tuple-element.87), channel_id=1, source_target_pairs={{8,0},{12,4},{16,8},{20,12},{24,16},{28,20},{32,24},{36,28},{40,32... | collective-permute-start | bytes 196616 | tf_op jit(solution)/shard_map/ppermute | solution.py:14
  411.1 5.6 %collective-permute-start.8 = (bf16[2,128,1,128]{3,1,0,2:T(8,128)(2,1)S(1)}, bf16[2,128,1,128]{3,1,0,2:T(8,128)(2,1)S(1)}, u32[]{:S(2)}, u32[]{:S(2)}) collective-permute-start(bf16[2,128,1,128]{3,1,0,2:T(8,128)(2,1)S(1)} %get-tuple-element.81), channel_id=1, source_target_pairs={{4,0},{8,4},{12,8},{16,12},{20,16},{24,20},{28,24},{32,28},{36,32}... | collective-permute-start | bytes 196616 | tf_op jit(solution)/shard_map/ppermute | solution.py:14
  (25 other events, 663.4 us)
Sparse Core Ops, SparseCore 0:
  11.0 184.1 all-gather.2
  251.8 32.9 reduce-scatter.3
  338.1 21.2 all-gather.4
where the time goes:
time: 427 us; the launch traced here: 425 us
  waiting for transfers between devices  192 us (45%)
  starting transfers between devices  97.6 us (23%)
  local copies, waits for them, and re-layouts  45.6 us (11%)
  other arithmetic  38.5 us (9%)
  matrix products  23.4 us (5%)
  between operations  14.7 us (3%)
  blocking collectives  12.9 us (3%)
    all_gather x1, waiting for transfers between devices, gather_columns(): half = lax.all_gather(out_weight, 'chip', axis=1, tiled=True)  135 us
    ppermute x14, starting transfers between devices, passed_along(): return lax.ppermute(array, axis, pairs)  55.1 us
    unnamed x4, waiting for transfers between devices  30.8 us
    all_to_all x1, starting transfers between devices, per_device(): lax.all_to_all(slot_grad.reshape(seq_count, capacity), 'seq', split_axis=...  18.3 us
    all_to_all x1, starting transfers between devices, per_device(): lax.all_to_all(payload.reshape(experts, capacity, features + 128), 'seq',...  18.2 us
    all_gather x1, waiting for transfers between devices, per_device(): input_grad = lax.all_gather(input_slice, 'head', axis=1, tiled=True)  17.5 us
    psum x1, blocking collectives, per_device(): slot_grad = lax.psum(slot_part, 'head')  12.9 us
    unnamed x73, local copies, waits for them, and re-layouts  11.7 us
  transfers between devices with their start and end apart: 20, of which 5 were waited for; matrix products, arithmetic and copies ran while one was open for 14% of the time, Pallas kernels for 0%

commit v1 on v0

--- a/solution.py
+++ b/solution.py
@@ -169,7 +169,10 @@
 
 
 def gather_columns(out_weight):
-    half = lax.all_gather(out_weight, "chip", axis=1, tiled=True)
+    half = jnp.concatenate(
+        lax.all_to_all(jnp.stack([out_weight] * lax.axis_size("chip"), axis=0), "chip", 0, 0),
+        axis=1,
+    )
     other = lax.ppermute(half, "core", [(0, 1), (1, 0)])
     return jnp.concatenate([half, other], axis=1)
 

time: 427 us -> 512 us (1.20)
  waiting for transfers between devices: 192 us -> 245 us
  starting transfers between devices: 97.6 us -> 130 us
    all_gather x1 -> x0, waiting for transfers between devices: 135 us -> none  [gather_columns(): half = lax.all_gather(out_weight, 'chip', axis=1, tiled=True)]
    all_to_all x1, waiting for transfers between devices: 0.01 us -> 97.9 us  [per_device(): lax.all_to_all(payload.reshape(experts, capacity, features + 128), 'seq',...]
    all_to_all x0 -> x1, waiting for transfers between devices: none -> 85.3 us  [gather_columns(): lax.all_to_all(jnp.stack([out_weight] * lax.axis_size('chip'), axis=0), '...]
    all_to_all x1, starting transfers between devices: 18.2 us -> 36.6 us  [per_device(): lax.all_to_all(payload.reshape(experts, capacity, features + 128), 'seq',...]
    all_to_all x0 -> x1, starting transfers between devices: none -> 16 us  [gather_columns(): lax.all_to_all(jnp.stack([out_weight] * lax.axis_size('chip'), axis=0), '...]
    unnamed x4 -> x3, waiting for transfers between devices: 30.8 us -> 36.1 us
    unnamed x73 -> x81, local copies, waits for them, and re-layouts: 11.7 us -> 11.5 us
  transfers between devices with their start and end apart: 20 -> 20, of which waited for: 5 -> 6; matrix products, arithmetic and copies ran while one was open for 14% -> 11% of each run, Pallas kernels for 0% -> 0%
where the time goes in v1:
time: 512 us; the launch traced here: 510 us
  waiting for transfers between devices  245 us (48%)
  starting transfers between devices  130 us (25%)
  local copies, waits for them, and re-layouts  48.8 us (10%)
  other arithmetic  35.6 us (7%)
  matrix products  22.6 us (4%)
  between operations  15 us (3%)
  blocking collectives  12.9 us (3%)
    all_to_all x1, waiting for transfers between devices, per_device(): lax.all_to_all(payload.reshape(experts, capacity, features + 128), 'seq',...  97.9 us
    all_to_all x1, waiting for transfers between devices, gather_columns(): lax.all_to_all(jnp.stack([out_weight] * lax.axis_size('chip'), axis=0), '...  85.3 us
    ppermute x14, starting transfers between devices, passed_along(): return lax.ppermute(array, axis, pairs)  56.6 us
    all_to_all x1, starting transfers between devices, per_device(): lax.all_to_all(payload.reshape(experts, capacity, features + 128), 'seq',...  36.6 us
    unnamed x3, waiting for transfers between devices  36.1 us
    all_to_all x1, starting transfers between devices, per_device(): lax.all_to_all(slot_grad.reshape(seq_count, capacity), 'seq', split_axis=...  18.3 us
    all_gather x1, waiting for transfers between devices, per_device(): input_grad = lax.all_gather(input_slice, 'head', axis=1, tiled=True)  17.6 us
    all_to_all x1, starting transfers between devices, gather_columns(): lax.all_to_all(jnp.stack([out_weight] * lax.axis_size('chip'), axis=0), '...  16 us
  transfers between devices with their start and end apart: 20, of which 6 were waited for; matrix products, arithmetic and copies ran while one was open for 11% of the time, Pallas kernels for 0%

profile of v1, /device:TPU:49, one launch (start us, length us, event | category | flops | bytes accessed | tf_op | source)
XLA Modules:
  0.0 510.3 jit_solution(14820125270549169203)
XLA Ops:
  10.7 16.0 %all-to-all-start = ((bf16[64,1024,32]{1,2,0:T(8,128)(2,1)}), bf16[64,1024,32]{1,2,0:T(8,128)(2,1)}, u32[]{:S(2)}, u32[]{:S(2)}) async-start(bf16[64,1024,32]{1,2,0:T(8,128)(2,1)} %stack.20), calls=%async_computation | async-start | bytes 8388608 | tf_op jit(solution)/shard_map/all_to_all | solution.py:173
  28.8 11.6 %convert_reduce_fusion = (bf16[1536,128]{1,0:T(8,128)(2,1)S(1)}, bf16[1536]{0:T(1024)(128)(2,1)S(1)}) fusion(s32[128,8]{0,1:T(8,128)S(1)} %convert_add_fusion, f32[128,8]{0,1:T(8,128)S(1)} %fusion.55), kind=kLoop, calls=%fused_computation.5 | loop fusion | flops 7666176 | bytes 404480 | tf_op jit(solution)/shard_map/reduce_sum | solution.py:78
  44.1 5.8 %copy.131 = bf16[1536,1152]{1,0:T(8,128)(2,1)} copy(bf16[1536,1152]{0,1:T(8,128)(2,1)} %fusion.6) | data formatting | bytes 7077888 | tf_op jit(solution)/shard_map/concatenate | solution.py:82
  49.9 6.5 %reshape.416 = bf16[128,12,1152]{2,1,0:T(8,128)(2,1)} reshape(bf16[1536,1152]{1,0:T(8,128)(2,1)} %copy.131) | data formatting | bytes 7077888 | tf_op jit(solution)/shard_map/reshape | solution.py:92
  56.4 85.3 %all-to-all-done = bf16[64,1024,32]{1,2,0:T(8,128)(2,1)} async-done(((bf16[64,1024,32]{1,2,0:T(8,128)(2,1)}), bf16[64,1024,32]{1,2,0:T(8,128)(2,1)}, u32[]{:S(2)}, u32[]{:S(2)}) %all-to-all-start) | async-done | bytes 4194336 | tf_op jit(solution)/shard_map/all_to_all | solution.py:173
  141.7 36.6 %all-to-all-start.1 = ((bf16[128,12,1152]{2,1,0:T(8,128)(2,1)}), bf16[128,12,1152]{2,1,0:T(8,128)(2,1)}, u32[]{:S(2)}, u32[]{:S(2)}) async-start(bf16[128,12,1152]{2,1,0:T(8,128)(2,1)} %reshape.416), calls=%async_computation.1 | async-start | bytes 9437184 | tf_op jit(solution)/shard_map/all_to_all | solution.py:91
  190.4 4.3 collective-permute-start.4
  194.7 97.9 %all-to-all-done.1 = bf16[128,12,1152]{2,1,0:T(8,128)(2,1)} async-done(((bf16[128,12,1152]{2,1,0:T(8,128)(2,1)}), bf16[128,12,1152]{2,1,0:T(8,128)(2,1)}, u32[]{:S(2)}, u32[]{:S(2)}) %all-to-all-start.1) | async-done | bytes 3538976 | tf_op jit(solution)/shard_map/all_to_all | solution.py:91
  292.7 6.6 %reshape.417 = bf16[1536,1152]{1,0:T(8,128)(2,1)} reshape(bf16[128,12,1152]{2,1,0:T(8,128)(2,1)} %all-to-all-done.1) | data formatting | bytes 7077888 | tf_op jit(solution)/shard_map/reshape | solution.py:97
  301.2 6.1 %collective-permute-start.6 = (bf16[2,128,1,128]{3,1,2,0:T(8,128)(2,1)S(1)}, bf16[2,128,1,128]{3,1,2,0:T(8,128)(2,1)S(1)}, u32[]{:S(2)}, u32[]{:S(2)}) collective-permute-start(bf16[2,128,1,128]{3,1,2,0:T(8,128)(2,1)S(1)} %pad_maximum_fusion.3), channel_id=1, source_target_pairs={{0,24},{4,28},{8,32},{12,36},{16,40},{20,44},{24,48},{28,52},{32,5... | collective-permute-start | bytes 196616 | tf_op jit(solution)/shard_map/ppermute | solution.py:14
  307.3 5.3 %collective-permute-start.7 = (bf16[2,128,1,128]{3,1,2,0:T(8,128)(2,1)S(1)}, bf16[2,128,1,128]{3,1,2,0:T(8,128)(2,1)S(1)}, u32[]{:S(2)}, u32[]{:S(2)}) collective-permute-start(bf16[2,128,1,128]{3,1,2,0:T(8,128)(2,1)S(1)} %pad_maximum_fusion.3), channel_id=1, source_target_pairs={{0,28},{4,32},{8,36},{12,40},{16,44},{20,48},{24,52},{28,56},{32,6... | collective-permute-start | bytes 196616 | tf_op jit(solution)/shard_map/ppermute | solution.py:14
  312.6 7.7 %pad_maximum_fusion = bf16[1024,4096]{0,1:T(8,128)(2,1)} fusion(bf16[1024,2048]{0,1:T(8,128)(2,1)} %collective-permute-done, bf16[1024,2048]{0,1:T(8,128)(2,1)} %bitcast.1), kind=kLoop, calls=%fused_computation.1 | loop fusion | flops 16777216 | bytes 16777216 | tf_op jit(solution)/shard_map/concatenate | solution.py:177
  320.4 6.1 %fusion.9 = bf16[768,1536]{0,1:T(8,128)(2,1)} fusion(bf16[1536,1152]{1,0:T(8,128)(2,1)} %reshape.417, bf16[1,768,1024]{2,1,0:T(8,128)(2,1)S(1)} %copy-done), kind=kOutput, calls=%fused_computation.21 | convolution fusion | flops 2417098752 | bytes 7077888 | tf_op jit(solution)/shard_map/dot_general | solution.py:105
  326.6 4.4 copy.155
  334.1 36.1 %reduce-scatter.4.cloned.1.call-done = bf16[192,1536]{1,0:T(8,128)(2,1)} async-done(((bf16[768,1536]{1,0:T(8,128)(2,1)}), bf16[192,1536]{1,0:T(8,128)(2,1)}) %reduce-scatter.4.cloned.1.call-update) | async-done | bytes 589840
  374.0 12.9 %psum.7 = f32[128,1,12]{2,0,1:T(8,128)} all-reduce(f32[128,1,12]{2,0,1:T(8,128)S(1)} %all_to_all.14), channel_id=1, replica_groups=mesh['chip'=64,'core'=2,'head'=4] {'head'}, use_global_device_ids=true, to_apply=%region_9.0 | all-reduce | flops 1536 | bytes 12288 | tf_op jit(solution)/shard_map/psum | solution.py:122
  386.9 18.3 %all-to-all-start.2 = ((f32[128,1,12]{2,1,0:T(1,128)}), f32[128,1,12]{2,1,0:T(1,128)S(1)}, u32[]{:S(2)}, u32[]{:S(2)}) async-start(f32[128,1,12]{2,1,0:T(1,128)} %bitcast.13), calls=%async_computation.2 | async-start | bytes 131072 | tf_op jit(solution)/shard_map/all_to_all | solution.py:123
  405.6 7.9 %all-to-all-done.2 = f32[128,1,12]{2,1,0:T(1,128)S(1)} async-done(((f32[128,1,12]{2,1,0:T(1,128)}), f32[128,1,12]{2,1,0:T(1,128)S(1)}, u32[]{:S(2)}, u32[]{:S(2)}) %all-to-all-start.2) | async-done | bytes 6176 | tf_op jit(solution)/shard_map/all_to_all | solution.py:123
  414.9 6.2 %gather_fusion = f32[1024]{0:T(1024)S(1)} fusion(f32[1536]{0:T(1024)S(1)} %reshape.418, s32[1024]{0:T(1024)S(1)} %broadcast_clamp_fusion), kind=kCustom, calls=%fused_computation | custom fusion | bytes 12288 | tf_op jit(solution)/shard_map/jit(_take)/gather | solution.py:126
  427.0 17.6 %all-gather.2.cloned.1.call-done = bf16[128,4096]{1,0:T(8,128)(2,1)} async-done(((bf16[128,1024]{1,0:T(8,128)(2,1)}), bf16[128,4096]{1,0:T(8,128)(2,1)}) %all-gather.2.cloned.1.call-update) | async-done | bytes 1048592 | tf_op jit(solution)/shard_map/all_gather | solution.py:131
  446.3 4.8 convolution_convert_fusion.2
  465.8 9.3 %collective-permute-start.14 = (bf16[2,128,1,128]{3,1,2,0:T(8,128)(2,1)}, bf16[2,128,1,128]{3,1,2,0:T(8,128)(2,1)}, u32[]{:S(2)}, u32[]{:S(2)}) collective-permute-start(bf16[2,128,1,128]{3,1,2,0:T(8,128)(2,1)} %get-tuple-element.82), channel_id=1, source_target_pairs={{28,0},{32,4},{36,8},{40,12},{44,16},{48,20},{52,24},{56,28},{60,3... | collective-permute-start | bytes 196616 | tf_op jit(solution)/shard_map/ppermute | solution.py:14
  481.0 5.2 %collective-permute-start.12 = (bf16[2,128,1,128]{3,1,0,2:T(8,128)(2,1)S(1)}, bf16[2,128,1,128]{3,1,0,2:T(8,128)(2,1)S(1)}, u32[]{:S(2)}, u32[]{:S(2)}) collective-permute-start(bf16[2,128,1,128]{3,1,0,2:T(8,128)(2,1)S(1)} %get-tuple-element.84), channel_id=1, source_target_pairs={{20,0},{24,4},{28,8},{32,12},{36,16},{40,20},{44,24},{48,28},{52,3... | collective-permute-start | bytes 196616 | tf_op jit(solution)/shard_map/ppermute | solution.py:14
  489.8 4.4 collective-permute-start.10
  (168 shorter events, 72.3 us)
Async XLA Ops:
  7.2 313.3 %copy-start = (bf16[1,768,1024]{2,1,0:T(8,128)(2,1)S(1)}, bf16[1,768,1024]{2,1,0:T(8,128)(2,1)}, u32[]{:S(2)}) copy-start(bf16[1,768,1024]{2,1,0:T(8,128)(2,1)} %param.19) | copy-start | bytes 4718596
  10.7 131.0 %all-to-all-start = ((bf16[64,1024,32]{1,2,0:T(8,128)(2,1)}), bf16[64,1024,32]{1,2,0:T(8,128)(2,1)}, u32[]{:S(2)}, u32[]{:S(2)}) async-start(bf16[64,1024,32]{1,2,0:T(8,128)(2,1)} %stack.20), calls=%async_computation | async-start | bytes 8388608 | tf_op jit(solution)/shard_map/all_to_all | solution.py:173
  56.4 124.2 %copy-start.27 = (bf16[128,1,128]{2,0,1:T(8,128)(2,1)S(1)}, bf16[128,1,128]{2,0,1:T(8,128)(2,1)}, u32[]{:S(2)}) copy-start(bf16[128,1,128]{2,0,1:T(8,128)(2,1)} %param.24) | copy-start | bytes 98308
  56.4 124.2 %copy-start.28 = (bf16[128,1,128]{2,0,1:T(8,128)(2,1)S(1)}, bf16[128,1,128]{2,0,1:T(8,128)(2,1)}, u32[]{:S(2)}) copy-start(bf16[128,1,128]{2,0,1:T(8,128)(2,1)} %param.23) | copy-start | bytes 98308
  141.7 151.0 %all-to-all-start.1 = ((bf16[128,12,1152]{2,1,0:T(8,128)(2,1)}), bf16[128,12,1152]{2,1,0:T(8,128)(2,1)}, u32[]{:S(2)}, u32[]{:S(2)}) async-start(bf16[128,12,1152]{2,1,0:T(8,128)(2,1)} %reshape.416), calls=%async_computation.1 | async-start | bytes 9437184 | tf_op jit(solution)/shard_map/all_to_all | solution.py:91
  178.3 191.8 %reduce-scatter.4.cloned.1.call-start = ((), (), s32[]{:S(2)}) async-start(), calls=%async_computation.5 | async-start | bytes 2949120
  178.4 129.0 %collective-permute-start = (bf16[1024,2048]{0,1:T(8,128)(2,1)}, bf16[1024,2048]{0,1:T(8,128)(2,1)}, u32[]{:S(2)}, u32[]{:S(2)}) collective-permute-start(bf16[1024,2048]{0,1:T(8,128)(2,1)} %bitcast.1), channel_id=1, source_target_pairs={{0,4},{4,0},{1,5},{5,1},{2,6},{6,2},{3,7},{7,3},{8,12},{12,8},{9,1... | collective-permute-start | bytes 12582920 | tf_op jit(solution)/shard_map/ppermute | solution.py:176
  180.7 118.6 %collective-permute-start.1 = (bf16[2,128,1,128]{3,1,2,0:T(8,128)(2,1)S(1)}, bf16[2,128,1,128]{3,1,2,0:T(8,128)(2,1)S(1)}, u32[]{:S(2)}, u32[]{:S(2)}) collective-permute-start(bf16[2,128,1,128]{3,1,2,0:T(8,128)(2,1)S(1)} %pad_maximum_fusion.3), channel_id=1, source_target_pairs={{0,4},{4,8},{8,12},{12,16},{16,20},{20,24},{24,28},{28,32},{32,36}... | collective-permute-start | bytes 196616 | tf_op jit(solution)/shard_map/ppermute | solution.py:14
  183.8 117.4 %collective-permute-start.2 = (bf16[2,128,1,128]{3,1,2,0:T(8,128)(2,1)S(1)}, bf16[2,128,1,128]{3,1,2,0:T(8,128)(2,1)S(1)}, u32[]{:S(2)}, u32[]{:S(2)}) collective-permute-start(bf16[2,128,1,128]{3,1,2,0:T(8,128)(2,1)S(1)} %pad_maximum_fusion.3), channel_id=1, source_target_pairs={{0,8},{4,12},{8,16},{12,20},{16,24},{20,28},{24,32},{28,36},{32,40... | collective-permute-start | bytes 196616 | tf_op jit(solution)/shard_map/ppermute | solution.py:14
  186.9 133.4 %collective-permute-start.3 = (bf16[2,128,1,128]{3,1,2,0:T(8,128)(2,1)S(1)}, bf16[2,128,1,128]{3,1,2,0:T(8,128)(2,1)S(1)}, u32[]{:S(2)}, u32[]{:S(2)}) collective-permute-start(bf16[2,128,1,128]{3,1,2,0:T(8,128)(2,1)S(1)} %pad_maximum_fusion.3), channel_id=1, source_target_pairs={{0,12},{4,16},{8,20},{12,24},{16,28},{20,32},{24,36},{28,40},{32,4... | collective-permute-start | bytes 196616 | tf_op jit(solution)/shard_map/ppermute | solution.py:14
  190.4 130.0 %collective-permute-start.4 = (bf16[2,128,1,128]{3,1,2,0:T(8,128)(2,1)S(1)}, bf16[2,128,1,128]{3,1,2,0:T(8,128)(2,1)S(1)}, u32[]{:S(2)}, u32[]{:S(2)}) collective-permute-start(bf16[2,128,1,128]{3,1,2,0:T(8,128)(2,1)S(1)} %pad_maximum_fusion.3), channel_id=1, source_target_pairs={{0,16},{4,20},{8,24},{12,28},{16,32},{20,36},{24,40},{28,44},{32,4... | collective-permute-start | bytes 196616 | tf_op jit(solution)/shard_map/ppermute | solution.py:14
  299.3 21.1 %collective-permute-start.5 = (bf16[2,128,1,128]{3,1,2,0:T(8,128)(2,1)S(1)}, bf16[2,128,1,128]{3,1,2,0:T(8,128)(2,1)S(1)}, u32[]{:S(2)}, u32[]{:S(2)}) collective-permute-start(bf16[2,128,1,128]{3,1,2,0:T(8,128)(2,1)S(1)} %pad_maximum_fusion.3), channel_id=1, source_target_pairs={{0,20},{4,24},{8,28},{12,32},{16,36},{20,40},{24,44},{28,48},{32,5... | collective-permute-start | bytes 196616 | tf_op jit(solution)/shard_map/ppermute | solution.py:14
  301.2 19.2 %collective-permute-start.6 = (bf16[2,128,1,128]{3,1,2,0:T(8,128)(2,1)S(1)}, bf16[2,128,1,128]{3,1,2,0:T(8,128)(2,1)S(1)}, u32[]{:S(2)}, u32[]{:S(2)}) collective-permute-start(bf16[2,128,1,128]{3,1,2,0:T(8,128)(2,1)S(1)} %pad_maximum_fusion.3), channel_id=1, source_target_pairs={{0,24},{4,28},{8,32},{12,36},{16,40},{20,44},{24,48},{28,52},{32,5... | collective-permute-start | bytes 196616 | tf_op jit(solution)/shard_map/ppermute | solution.py:14
  307.3 13.1 %collective-permute-start.7 = (bf16[2,128,1,128]{3,1,2,0:T(8,128)(2,1)S(1)}, bf16[2,128,1,128]{3,1,2,0:T(8,128)(2,1)S(1)}, u32[]{:S(2)}, u32[]{:S(2)}) collective-permute-start(bf16[2,128,1,128]{3,1,2,0:T(8,128)(2,1)S(1)} %pad_maximum_fusion.3), channel_id=1, source_target_pairs={{0,28},{4,32},{8,36},{12,40},{16,44},{20,48},{24,52},{28,56},{32,6... | collective-permute-start | bytes 196616 | tf_op jit(solution)/shard_map/ppermute | solution.py:14
  371.5 50.6 %copy-start.9 = (bf16[128,1024]{1,0:T(8,128)(2,1)S(1)}, bf16[128,1024]{1,0:T(8,128)(2,1)}, u32[]{:S(2)}) copy-start(bf16[128,1024]{1,0:T(8,128)(2,1)} %param.14) | copy-start | bytes 786436
  386.9 26.6 %all-to-all-start.2 = ((f32[128,1,12]{2,1,0:T(1,128)}), f32[128,1,12]{2,1,0:T(1,128)S(1)}, u32[]{:S(2)}, u32[]{:S(2)}) async-start(f32[128,1,12]{2,1,0:T(1,128)} %bitcast.13), calls=%async_computation.2 | async-start | bytes 131072 | tf_op jit(solution)/shard_map/all_to_all | solution.py:123
  405.3 39.3 %all-gather.2.cloned.1.call-start = ((), (), s32[]{:S(2)}) async-start(), calls=%async_computation.4 | async-start | bytes 1310720 | tf_op jit(solution)/shard_map/all_gather | solution.py:131
  465.8 28.4 %collective-permute-start.14 = (bf16[2,128,1,128]{3,1,2,0:T(8,128)(2,1)}, bf16[2,128,1,128]{3,1,2,0:T(8,128)(2,1)}, u32[]{:S(2)}, u32[]{:S(2)}) collective-permute-start(bf16[2,128,1,128]{3,1,2,0:T(8,128)(2,1)} %get-tuple-element.82), channel_id=1, source_target_pairs={{28,0},{32,4},{36,8},{40,12},{44,16},{48,20},{52,24},{56,28},{60,3... | collective-permute-start | bytes 196616 | tf_op jit(solution)/shard_map/ppermute | solution.py:14
  475.1 21.1 %collective-permute-start.13 = (bf16[2,128,1,128]{3,1,0,2:T(8,128)(2,1)S(1)}, bf16[2,128,1,128]{3,1,0,2:T(8,128)(2,1)}, u32[]{:S(2)}, u32[]{:S(2)}) collective-permute-start(bf16[2,128,1,128]{3,1,0,2:T(8,128)(2,1)S(1)} %get-tuple-element.83), channel_id=1, source_target_pairs={{24,0},{28,4},{32,8},{36,12},{40,16},{44,20},{48,24},{52,28},{56,3... | collective-permute-start | bytes 196616 | tf_op jit(solution)/shard_map/ppermute | solution.py:14
  481.0 20.5 %collective-permute-start.12 = (bf16[2,128,1,128]{3,1,0,2:T(8,128)(2,1)S(1)}, bf16[2,128,1,128]{3,1,0,2:T(8,128)(2,1)S(1)}, u32[]{:S(2)}, u32[]{:S(2)}) collective-permute-start(bf16[2,128,1,128]{3,1,0,2:T(8,128)(2,1)S(1)} %get-tuple-element.84), channel_id=1, source_target_pairs={{20,0},{24,4},{28,8},{32,12},{36,16},{40,20},{44,24},{48,28},{52,3... | collective-permute-start | bytes 196616 | tf_op jit(solution)/shard_map/ppermute | solution.py:14
  486.1 15.3 %collective-permute-start.11 = (bf16[2,128,1,128]{3,1,0,2:T(8,128)(2,1)S(1)}, bf16[2,128,1,128]{3,1,0,2:T(8,128)(2,1)S(1)}, u32[]{:S(2)}, u32[]{:S(2)}) collective-permute-start(bf16[2,128,1,128]{3,1,0,2:T(8,128)(2,1)S(1)} %get-tuple-element.85), channel_id=1, source_target_pairs={{16,0},{20,4},{24,8},{28,12},{32,16},{36,20},{40,24},{44,28},{48,3... | collective-permute-start | bytes 196616 | tf_op jit(solution)/shard_map/ppermute | solution.py:14
  489.8 11.7 %collective-permute-start.10 = (bf16[2,128,1,128]{3,1,0,2:T(8,128)(2,1)S(1)}, bf16[2,128,1,128]{3,1,0,2:T(8,128)(2,1)S(1)}, u32[]{:S(2)}, u32[]{:S(2)}) collective-permute-start(bf16[2,128,1,128]{3,1,0,2:T(8,128)(2,1)S(1)} %get-tuple-element.86), channel_id=1, source_target_pairs={{12,0},{16,4},{20,8},{24,12},{28,16},{32,20},{36,24},{40,28},{44,3... | collective-permute-start | bytes 196616 | tf_op jit(solution)/shard_map/ppermute | solution.py:14
  494.2 7.3 %collective-permute-start.9 = (bf16[2,128,1,128]{3,1,0,2:T(8,128)(2,1)S(1)}, bf16[2,128,1,128]{3,1,0,2:T(8,128)(2,1)S(1)}, u32[]{:S(2)}, u32[]{:S(2)}) collective-permute-start(bf16[2,128,1,128]{3,1,0,2:T(8,128)(2,1)S(1)} %get-tuple-element.87), channel_id=1, source_target_pairs={{8,0},{12,4},{16,8},{20,12},{24,16},{28,20},{32,24},{36,28},{40,32... | collective-permute-start | bytes 196616 | tf_op jit(solution)/shard_map/ppermute | solution.py:14
  496.2 5.6 %collective-permute-start.8 = (bf16[2,128,1,128]{3,1,0,2:T(8,128)(2,1)S(1)}, bf16[2,128,1,128]{3,1,0,2:T(8,128)(2,1)S(1)}, u32[]{:S(2)}, u32[]{:S(2)}) collective-permute-start(bf16[2,128,1,128]{3,1,0,2:T(8,128)(2,1)S(1)} %get-tuple-element.81), channel_id=1, source_target_pairs={{4,0},{8,4},{12,8},{16,12},{20,16},{24,20},{28,24},{32,28},{36,32}... | collective-permute-start | bytes 196616 | tf_op jit(solution)/shard_map/ppermute | solution.py:14
  (29 other events, 726.5 us)
Sparse Core Ops, SparseCore 0:
  331.1 38.9 reduce-scatter.3
  423.3 21.2 all-gather.1
